TPU v7x, 256 devices: a whole 4x4x8 slice. The times are simulated.
256 devices in a mesh: mem: 4 (over x), col: 64 (over y, z, core).
Axes of the slice: x: 4, y: 4, z: 8, core: 2. Of those that a mesh axis runs over, the one named last changes fastest.
Arguments:
- perturbations: bfloat16 [32, 256, 256, 128], P('mem', 'col'), may hold values from -4 to 4
- static_root: float32 [128, 128], replicated, may hold values from -0.5 to 1.5
- obs_jacobian: float32 [128, 128], replicated, may hold values from -0.5 to 0.5
- innovations: float32 [16384, 128], P('col'), may hold values from -6 to 6
- obs_weights: float32 [128], replicated, may hold values from 0.2 to 2
- length_scale: float32 [256, 256], P('col'), may hold values from 0.05 to 0.24
- obs_owner: int32 [16384, 1], P('col'), may hold values from 0 to 63; in each aligned block of 256 rows (0 to 255, 256 to 511, ...) at most 8 rows name the same one
- obs_cell: int32 [16384], P('col'), may hold values from 0 to 1023
- obs_count: int32 [64], P('col'), may hold values from 128 to 256, as said below
Outputs:
- increment: float32 [256, 256, 128], P('col', 'mem')
- control_static: float32 [256, 256, 128], P('col', 'mem')
- control_ensemble: float32 [32, 256, 256], P('mem', 'col')
Inputs may be any that keep to these rules, and one draw needn't show every extreme that they name: `obs_owner`: each holder's 256 rows name any one column block at most 8 times. `obs_count`: rows at or past a holder's count are padding and are ignored; at least one holder is full. `obs_cell`: the column within the owner's block, numbered y * 256 + x, where y is its grid row within the block (0 to 3).
All inputs are finite; a program needn't handle non-finite values.
Results may differ from a plain program's by a relative error of at most 0.004.
Values may be sent and summed in bfloat16 or wider, within the bound.
No kernel may reach another device: no remote copies, remote signals or barrier semaphores. Data moves between devices by JAX's collectives and lax.ppermute only.
A program may use at most 64 MiB of HBM per device.

v0:
```python
import jax
import jax.numpy as jnp
from jax import lax
from jax.sharding import PartitionSpec as P

NSWEEP = 4
ITERS = 2


def extended(block, sides, width):
    for axis, dim in sides:
        count = lax.axis_size(axis)
        forward = [(i, i + 1) for i in range(count - 1)]
        backward = [(target, source) for source, target in forward]
        low = lax.ppermute(
            lax.slice_in_dim(block, block.shape[dim] - width, None, axis=dim), axis, forward
        )
        high = lax.ppermute(lax.slice_in_dim(block, 0, width, axis=dim), axis, backward)
        block = jnp.concatenate([low, block, high], axis=dim)
    return block


def face_coefficients(length_scale):
    rimmed = extended(length_scale, (("col", 0),), 1)
    padded = jnp.pad(rimmed, ((0, 0), (1, 1)))
    return (
        jnp.sqrt(length_scale * padded[:-2, 1:-1]),
        jnp.sqrt(length_scale * padded[2:, 1:-1]),
        jnp.sqrt(length_scale * padded[1:-1, :-2]),
        jnp.sqrt(length_scale * padded[1:-1, 2:]),
    )


def sweeps(values, coeffs):
    face_up, face_down, face_left, face_right = coeffs
    for sweep_step in range(NSWEEP):
        rimmed = extended(values, (("col", 1),), 1)
        padded = jnp.pad(rimmed, ((0, 0), (0, 0), (1, 1)))
        centre = values
        values = (
            centre
            + face_up * (padded[:, :-2, 1:-1] - centre)
            + face_down * (padded[:, 2:, 1:-1] - centre)
            + face_left * (padded[:, 1:-1, :-2] - centre)
            + face_right * (padded[:, 1:-1, 2:] - centre)
        )
    return values


def local_inner(first, second):
    return jnp.sum(first[0] * second[0]) + jnp.sum(first[1] * second[1])


def shards(
    perturbations,
    static_root,
    obs_jacobian,
    innovations,
    obs_weights,
    length_scale,
    obs_owner,
    obs_cell,
    obs_count,
):
    members, rows_here, columns, features = perturbations.shape
    quarter = columns // lax.axis_size("mem")
    offset = lax.axis_index("mem") * quarter
    blocks = lax.axis_size("col")
    obs_dev, channels = innovations.shape
    capacity = max(2, 2 * obs_dev // blocks)
    total_slots = blocks * capacity
    coeffs = face_coefficients(length_scale)
    is_live = jnp.arange(obs_dev, dtype=jnp.int32) < obs_count[0]
    owner_ids = obs_owner[:, 0]
    onehot = (
        (owner_ids[:, None] == jnp.arange(blocks, dtype=jnp.int32)[None, :]) & is_live[:, None]
    ).astype(jnp.int32)
    slot_rank = jnp.sum((jnp.cumsum(onehot, axis=0) - onehot) * onehot, axis=1)
    slot_ids = jnp.where(is_live, owner_ids * capacity + slot_rank, total_slots)
    send_values = (
        jnp.zeros((total_slots, channels), jnp.float32).at[slot_ids].set(innovations, mode="drop")
    )
    send_cells = jnp.zeros((total_slots,), jnp.int32).at[slot_ids].set(obs_cell, mode="drop")
    send_marks = jnp.zeros((total_slots,), jnp.float32).at[slot_ids].set(1.0, mode="drop")
    got_values, got_cells, got_marks = (
        lax.all_to_all(
            send_values.reshape(blocks, capacity, channels),
            "col",
            split_axis=0,
            concat_axis=0,
            tiled=True,
        ),
        lax.all_to_all(
            send_cells.reshape(blocks, capacity), "col", split_axis=0, concat_axis=0, tiled=True
        ),
        lax.all_to_all(
            send_marks.reshape(blocks, capacity), "col", split_axis=0, concat_axis=0, tiled=True
        ),
    )
    got_values = got_values.reshape(total_slots, channels)
    got_cells = got_cells.reshape(total_slots)
    got_marks = got_marks.reshape(total_slots)
    obs_index = got_cells
    obs_gain = got_marks[:, None] * obs_weights[None, :]

    def spread_back(weighted):
        back = jnp.dot(weighted, obs_jacobian.T, precision=lax.Precision.HIGHEST)
        grid = jnp.zeros((rows_here * columns, features), jnp.float32).at[obs_index].add(back)
        return grid.reshape(rows_here, columns, features)

    def adjoint_map(gradient):
        own_gradient = lax.dynamic_slice_in_dim(gradient, offset, quarter, 1)
        rounded = gradient.astype(jnp.bfloat16)
        static = jnp.dot(
            own_gradient.reshape(rows_here * quarter, features),
            static_root.T,
            precision=lax.Precision.HIGHEST,
        ).reshape(rows_here, quarter, features)
        projected = jnp.einsum(
            "kyxf,yxf->kyx", perturbations, rounded, preferred_element_type=jnp.float32
        )
        return (static, sweeps(projected, coeffs))

    residual = adjoint_map(spread_back(obs_gain * got_values))
    direction = residual
    state = (jnp.zeros_like(residual[0]), jnp.zeros_like(residual[1]))
    increment = jnp.zeros((rows_here, quarter, features), jnp.float32)
    norm_now = lax.psum(local_inner(residual, residual), ("mem", "col"))
    for iteration in range(ITERS):
        smoothed = sweeps(direction[1], coeffs).astype(jnp.bfloat16)
        partial_sum = jnp.einsum(
            "kyxf,kyx->yxf", perturbations, smoothed, preferred_element_type=jnp.float32
        )
        forward_static = jnp.dot(
            direction[0].reshape(rows_here * quarter, features),
            static_root,
            precision=lax.Precision.HIGHEST,
        ).reshape(rows_here, quarter, features)
        own_slice = lax.dynamic_slice_in_dim(partial_sum, offset, quarter, 1) + forward_static
        partial_sum = lax.dynamic_update_slice_in_dim(partial_sum, own_slice, offset, 1)
        image_part = lax.psum(partial_sum, "mem")
        own_image = lax.dynamic_slice_in_dim(image_part, offset, quarter, 1)
        image_part, own_image = (image_part, own_image)
        gathered = image_part.reshape(rows_here * columns, features)[obs_index]
        model_obs = jnp.dot(gathered, obs_jacobian, precision=lax.Precision.HIGHEST)
        adj_static, adj_ensemble = adjoint_map(spread_back(obs_gain * model_obs))
        image = (direction[0] + adj_static, direction[1] + adj_ensemble)
        step = norm_now / lax.psum(local_inner(direction, image), ("mem", "col"))
        residual = (residual[0] - step * image[0], residual[1] - step * image[1])
        norm_next = lax.psum(local_inner(residual, residual), ("mem", "col"))
        state = (state[0] + step * direction[0], state[1] + step * direction[1])
        increment = increment + step * own_image
        ratio = norm_next / norm_now
        direction = (residual[0] + ratio * direction[0], residual[1] + ratio * direction[1])
        norm_now = norm_next
    return (increment, state[0], state[1])


def solution(mesh):
    placed = (
        P("mem", "col", None, None),
        P(),
        P(),
        P("col", None),
        P(),
        P("col", None),
        P("col", None),
        P("col"),
        P("col"),
    )
    return jax.shard_map(
        shards,
        mesh=mesh,
        in_specs=placed,
        out_specs=(P("col", "mem", None), P("col", "mem", None), P("mem", "col", None)),
        check_vma=False,
    )
```

profile of v0, /device:TPU:1, one launch (start us, length us, event | category | flops | bytes accessed | tf_op | source)
XLA Modules:
  0.0 626.9 jit_solution(7078985824332760388)
XLA Ops:
  13.3 13.1 %all-to-all-start = ((s32[64,1,8]{2,1,0:T(1,128)}), s32[64,1,8]{2,1,0:T(1,128)S(1)}, u32[]{:S(2)}, u32[]{:S(2)}) async-start(s32[64,1,8]{2,1,0:T(1,128)} %bitcast.6), calls=%async_computation | async-start | bytes 65536 | tf_op jit(solution)/shard_map/all_to_all | solution.py:93
  28.5 7.1 %all-to-all-done = s32[64,1,8]{2,1,0:T(1,128)S(1)} async-done(((s32[64,1,8]{2,1,0:T(1,128)}), s32[64,1,8]{2,1,0:T(1,128)S(1)}, u32[]{:S(2)}, u32[]{:S(2)}) %all-to-all-start) | async-done | bytes 2080 | tf_op jit(solution)/shard_map/all_to_all | solution.py:93
  35.7 4.7 all-to-all-start.1
  42.5 7.2 %all-to-all-done.1 = f32[64,1,8]{2,1,0:T(1,128)S(1)} async-done(((f32[64,1,8]{2,1,0:T(1,128)}), f32[64,1,8]{2,1,0:T(1,128)S(1)}, u32[]{:S(2)}, u32[]{:S(2)}) %all-to-all-start.1) | async-done | bytes 2080 | tf_op jit(solution)/shard_map/all_to_all | solution.py:96
  49.7 4.7 all-to-all-start.2
  55.3 3.5 collective-permute-start
  60.7 3.2 collective-permute-done.2
  73.1 3.3 collective-permute-start.1
  78.4 2.9 collective-permute-done.3
  100.7 4.8 collective-permute-done.9
  110.3 3.8 collective-permute-done.11
  118.7 3.8 collective-permute-done.13
  142.6 54.8 %all-reduce.25.cloned.1.call-done = f32[4,256,128]{2,1,0:T(8,128)} async-done(((f32[4,256,128]{2,1,0:T(8,128)}), f32[4,256,128]{2,1,0:T(8,128)}) %all-reduce.25.cloned.1.call-update) | async-done | bytes 524304 | tf_op jit(solution)/shard_map/psum | solution.py:141
  206.3 6.9 %collective-permute-start.18 = (f32[8,1,256]{2,1,0:T(1,128)S(1)}, f32[8,1,256]{2,1,0:T(1,128)S(1)}, u32[]{:S(2)}, u32[]{:S(2)}) collective-permute-start(f32[8,1,256]{2,1,0:T(1,128)S(1)} %get-tuple-element.30), channel_id=1, source_target_pairs={{0,1},{1,2},{2,3},{3,4},{4,5},{5,6},{6,7},{7,8},{8,9},{9,10},{10,1... | collective-permute-start | bytes 24584 | tf_op jit(solution)/shard_map/ppermute | solution.py:15
  215.1 3.0 collective-permute-done.19
  238.0 3.9 collective-permute-done.25
  245.4 80.6 %all-reduce.21 = (f32[]{:T(128)}, f32[]{:T(128)}) all-reduce(f32[]{:T(128)S(6)} %add.401, f32[]{:T(128)S(6)} %add.437), channel_id=1, replica_groups=mesh['mem'=4,'col'=64] {'mem','col'}, use_global_device_ids=true, to_apply=%region_9.10 | all-reduce | flops 2 | bytes 16 | tf_op jit(solution)/shard_map/psum | solution.py:128
  329.9 73.2 %psum.45 = f32[]{:T(128)} all-reduce(f32[]{:T(128)S(6)} %add.438), channel_id=1, replica_groups=mesh['mem'=4,'col'=64] {'mem','col'}, use_global_device_ids=true, to_apply=%region_17.18 | all-reduce | flops 1 | bytes 8 | tf_op jit(solution)/shard_map/psum | solution.py:150
  404.4 4.2 collective-permute-start.26
  440.4 48.7 %all-reduce.27.cloned.1.call-done = f32[4,256,128]{2,1,0:T(8,128)} async-done(((f32[4,256,128]{2,1,0:T(8,128)}), f32[4,256,128]{2,1,0:T(8,128)}) %all-reduce.27.cloned.1.call-update) | async-done | bytes 524304 | tf_op jit(solution)/shard_map/psum | solution.py:141
  498.1 6.8 %collective-permute-start.34 = (f32[8,1,256]{2,1,0:T(1,128)S(1)}, f32[8,1,256]{2,1,0:T(1,128)S(1)}, u32[]{:S(2)}, u32[]{:S(2)}) collective-permute-start(f32[8,1,256]{2,1,0:T(1,128)S(1)} %get-tuple-element.14), channel_id=1, source_target_pairs={{0,1},{1,2},{2,3},{3,4},{4,5},{5,6},{6,7},{7,8},{8,9},{9,10},{10,1... | collective-permute-start | bytes 24584 | tf_op jit(solution)/shard_map/ppermute | solution.py:15
  506.9 3.0 collective-permute-done.35
  529.8 4.0 collective-permute-done.41
  535.9 80.6 %psum.47 = f32[]{:T(128)} all-reduce(f32[]{:T(128)S(6)} %add.476), channel_id=1, replica_groups=mesh['mem'=4,'col'=64] {'mem','col'}, use_global_device_ids=true, to_apply=%region_22.23 | all-reduce | flops 1 | bytes 8 | tf_op jit(solution)/shard_map/psum | solution.py:148
  (212 shorter events, 169.8 us)
Async XLA Ops:
  13.3 22.4 %all-to-all-start = ((s32[64,1,8]{2,1,0:T(1,128)}), s32[64,1,8]{2,1,0:T(1,128)S(1)}, u32[]{:S(2)}, u32[]{:S(2)}) async-start(s32[64,1,8]{2,1,0:T(1,128)} %bitcast.6), calls=%async_computation | async-start | bytes 65536 | tf_op jit(solution)/shard_map/all_to_all | solution.py:93
  35.7 14.1 %all-to-all-start.1 = ((f32[64,1,8]{2,1,0:T(1,128)}), f32[64,1,8]{2,1,0:T(1,128)S(1)}, u32[]{:S(2)}, u32[]{:S(2)}) async-start(f32[64,1,8]{2,1,0:T(1,128)} %bitcast.8), calls=%async_computation.1 | async-start | bytes 65536 | tf_op jit(solution)/shard_map/all_to_all | solution.py:96
  49.7 17.7 %all-to-all-start.2 = ((f32[64,8,128]{2,1,0:T(8,128)}), f32[64,8,128]{2,1,0:T(8,128)S(1)}, u32[]{:S(2)}, u32[]{:S(2)}) async-start(f32[64,8,128]{2,1,0:T(8,128)} %bitcast.9), calls=%async_computation.2 | async-start | bytes 524288 | tf_op jit(solution)/shard_map/all_to_all | solution.py:86
  54.4 142.9 %all-reduce.25.cloned.1.call-start = ((), (), s32[]{:S(2)}) async-start(), calls=%async_computation.3 | async-start | bytes 1048576 | tf_op jit(solution)/shard_map/psum | solution.py:141
  55.3 5.5 collective-permute-start
  58.8 5.2 collective-permute-start.2
  73.1 5.3 collective-permute-start.1
  76.4 5.0 collective-permute-start.3
  90.8 5.2 collective-permute-start.7
  98.3 7.2 %collective-permute-start.9 = (f32[8,1,256]{2,1,0:T(1,128)S(1)}, f32[8,1,256]{2,1,0:T(1,128)S(1)}, u32[]{:S(2)}, u32[]{:S(2)}) collective-permute-start(f32[8,1,256]{2,1,0:T(1,128)S(1)} %get-tuple-element.41), channel_id=1, source_target_pairs={{1,0},{2,1},{3,2},{4,3},{5,4},{6,5},{7,6},{8,7},{9,8},{10,9},{11,1... | collective-permute-start | bytes 24584 | tf_op jit(solution)/shard_map/ppermute | solution.py:18
  107.9 6.2 collective-permute-start.11
  116.3 6.2 collective-permute-start.13
  122.7 5.2 collective-permute-start.14
  124.7 6.2 collective-permute-start.15
  131.1 5.3 collective-permute-start.16
  133.1 6.2 collective-permute-start.17
  142.5 346.6 %all-reduce.27.cloned.1.call-start = ((), (), s32[]{:S(2)}) async-start(), calls=%async_computation.4 | async-start | bytes 1048576 | tf_op jit(solution)/shard_map/psum | solution.py:141
  206.3 8.8 %collective-permute-start.18 = (f32[8,1,256]{2,1,0:T(1,128)S(1)}, f32[8,1,256]{2,1,0:T(1,128)S(1)}, u32[]{:S(2)}, u32[]{:S(2)}) collective-permute-start(f32[8,1,256]{2,1,0:T(1,128)S(1)} %get-tuple-element.30), channel_id=1, source_target_pairs={{0,1},{1,2},{2,3},{3,4},{4,5},{5,6},{6,7},{7,8},{8,9},{9,10},{10,1... | collective-permute-start | bytes 24584 | tf_op jit(solution)/shard_map/ppermute | solution.py:15
  232.8 5.2 collective-permute-start.24
  234.8 7.2 %collective-permute-start.25 = (f32[8,1,256]{2,1,0:T(1,128)S(1)}, f32[8,1,256]{2,1,0:T(1,128)S(1)}, u32[]{:S(2)}, u32[]{:S(2)}) collective-permute-start(f32[8,1,256]{2,1,0:T(1,128)S(1)} %get-tuple-element.25), channel_id=1, source_target_pairs={{1,0},{2,1},{3,2},{4,3},{5,4},{6,5},{7,6},{8,7},{9,8},{10,9},{11,1... | collective-permute-start | bytes 24584 | tf_op jit(solution)/shard_map/ppermute | solution.py:18
  404.4 6.4 %collective-permute-start.26 = (f32[8,1,256]{2,1,0:T(1,128)S(1)}, f32[8,1,256]{2,1,0:T(1,128)S(1)}, u32[]{:S(2)}, u32[]{:S(2)}) collective-permute-start(f32[8,1,256]{2,1,0:T(1,128)S(1)} %get-tuple-element.22), channel_id=1, source_target_pairs={{0,1},{1,2},{2,3},{3,4},{4,5},{5,6},{6,7},{7,8},{8,9},{9,10},{10,1... | collective-permute-start | bytes 24584 | tf_op jit(solution)/shard_map/ppermute | solution.py:15
  498.1 8.8 %collective-permute-start.34 = (f32[8,1,256]{2,1,0:T(1,128)S(1)}, f32[8,1,256]{2,1,0:T(1,128)S(1)}, u32[]{:S(2)}, u32[]{:S(2)}) collective-permute-start(f32[8,1,256]{2,1,0:T(1,128)S(1)} %get-tuple-element.14), channel_id=1, source_target_pairs={{0,1},{1,2},{2,3},{3,4},{4,5},{5,6},{6,7},{7,8},{8,9},{9,10},{10,1... | collective-permute-start | bytes 24584 | tf_op jit(solution)/shard_map/ppermute | solution.py:15
  524.6 5.2 collective-permute-start.40
  526.5 7.2 %collective-permute-start.41 = (f32[8,1,256]{2,1,0:T(1,128)S(1)}, f32[8,1,256]{2,1,0:T(1,128)S(1)}, u32[]{:S(2)}, u32[]{:S(2)}) collective-permute-start(f32[8,1,256]{2,1,0:T(1,128)S(1)} %get-tuple-element.9), channel_id=1, source_target_pairs={{1,0},{2,1},{3,2},{4,3},{5,4},{6,5},{7,6},{8,7},{9,8},{10,9},{11,1... | collective-permute-start | bytes 24584 | tf_op jit(solution)/shard_map/ppermute | solution.py:18
  (31 other events, 351.4 us)
Sparse Core Ops, SparseCore 0:
  142.7 54.6 all-reduce.24
  440.6 48.5 all-reduce.26
where the time goes:
time: 629 us; the launch traced here: 627 us
  blocking collectives  234 us (37%)
  waiting for transfers between devices  182 us (29%)
  starting transfers between devices  127 us (20%)
  between operations  25.3 us (4%)
  other arithmetic  22.1 us (4%)
  local copies, waits for them, and re-layouts  18.9 us (3%)
  matrix products  17.4 us (3%)
    psum x2, waiting for transfers between devices, shards(): image_part = lax.psum(partial_sum, 'mem')  104 us
    psum x1, blocking collectives, shards(): norm_now = lax.psum(local_inner(residual, residual), ('mem', 'col'))  80.6 us
    psum x1, blocking collectives, shards(): step = norm_now / lax.psum(local_inner(direction, image), ('mem', 'col'))  80.6 us
    psum x1, blocking collectives, shards(): norm_next = lax.psum(local_inner(residual, residual), ('mem', 'col'))  73.2 us
    ppermute x21, waiting for transfers between devices, extended(): lax.ppermute(lax.slice_in_dim(block, 0, width, axis=dim), axis, backward)  64.5 us
    ppermute x21, starting transfers between devices, extended(): lax.ppermute(lax.slice_in_dim(block, block.shape[dim] - width, None, axis...  56 us
    ppermute x21, starting transfers between devices, extended(): lax.ppermute(lax.slice_in_dim(block, 0, width, axis=dim), axis, backward)  47.9 us
    all_to_all x1, starting transfers between devices, shards(): lax.all_to_all(send_cells.reshape(blocks, capacity), 'col', split_axis=0,...  13.1 us
  transfers between devices with their start and end apart: 47, of which 25 were waited for; matrix products, arithmetic and copies ran while one was open for 2% of the time, Pallas kernels for 0%

commit v1 on v0

--- a/solution.py
+++ b/solution.py
@@ -138,7 +138,7 @@
         ).reshape(rows_here, quarter, features)
         own_slice = lax.dynamic_slice_in_dim(partial_sum, offset, quarter, 1) + forward_static
         partial_sum = lax.dynamic_update_slice_in_dim(partial_sum, own_slice, offset, 1)
-        image_part = lax.psum(partial_sum, "mem")
+        image_part = jnp.sum(lax.all_gather(partial_sum, "mem"), axis=0)
         own_image = lax.dynamic_slice_in_dim(image_part, offset, quarter, 1)
         image_part, own_image = (image_part, own_image)
         gathered = image_part.reshape(rows_here * columns, features)[obs_index]

time: 629 us -> 609 us (0.968)
  waiting for transfers between devices: 182 us -> 156 us
  other arithmetic: 22.1 us -> 29.4 us
    psum x2 -> x0, waiting for transfers between devices: 104 us -> none  [shards(): image_part = lax.psum(partial_sum, 'mem')]
    all_gather x0 -> x2, waiting for transfers between devices: none -> 77.5 us  [shards(): image_part = jnp.sum(lax.all_gather(partial_sum, 'mem'), axis=0)]
where the time goes in v1:
time: 609 us; the launch traced here: 606 us
  blocking collectives  234 us (38%)
  waiting for transfers between devices  156 us (26%)
  starting transfers between devices  122 us (20%)
  other arithmetic  29.4 us (5%)
  between operations  25.2 us (4%)
  matrix products  19.9 us (3%)
  local copies, waits for them, and re-layouts  19.2 us (3%)
    psum x1, blocking collectives, shards(): norm_now = lax.psum(local_inner(residual, residual), ('mem', 'col'))  80.5 us
    psum x1, blocking collectives, shards(): step = norm_now / lax.psum(local_inner(direction, image), ('mem', 'col'))  80.4 us
    all_gather x2, waiting for transfers between devices, shards(): image_part = jnp.sum(lax.all_gather(partial_sum, 'mem'), axis=0)  77.5 us
    psum x1, blocking collectives, shards(): norm_next = lax.psum(local_inner(residual, residual), ('mem', 'col'))  72.7 us
    ppermute x21, waiting for transfers between devices, extended(): lax.ppermute(lax.slice_in_dim(block, 0, width, axis=dim), axis, backward)  64.4 us
    ppermute x21, starting transfers between devices, extended(): lax.ppermute(lax.slice_in_dim(block, block.shape[dim] - width, None, axis...  51.9 us
    ppermute x21, starting transfers between devices, extended(): lax.ppermute(lax.slice_in_dim(block, 0, width, axis=dim), axis, backward)  47.9 us
    all_to_all x1, starting transfers between devices, shards(): lax.all_to_all(send_cells.reshape(blocks, capacity), 'col', split_axis=0,...  13.1 us
  transfers between devices with their start and end apart: 47, of which 25 were waited for; matrix products, arithmetic and copies ran while one was open for 2% of the time, Pallas kernels for 0%

profile of v1, /device:TPU:1, one launch (start us, length us, event | category | flops | bytes accessed | tf_op | source)
XLA Modules:
  0.0 606.1 jit_solution(3850877065599096292)
XLA Ops:
  13.3 13.1 %all-to-all-start = ((s32[64,1,8]{2,1,0:T(1,128)}), s32[64,1,8]{2,1,0:T(1,128)S(1)}, u32[]{:S(2)}, u32[]{:S(2)}) async-start(s32[64,1,8]{2,1,0:T(1,128)} %bitcast.6), calls=%async_computation | async-start | bytes 65536 | tf_op jit(solution)/shard_map/all_to_all | solution.py:93
  28.5 7.1 %all-to-all-done = s32[64,1,8]{2,1,0:T(1,128)S(1)} async-done(((s32[64,1,8]{2,1,0:T(1,128)}), s32[64,1,8]{2,1,0:T(1,128)S(1)}, u32[]{:S(2)}, u32[]{:S(2)}) %all-to-all-start) | async-done | bytes 2080 | tf_op jit(solution)/shard_map/all_to_all | solution.py:93
  35.7 4.7 all-to-all-start.1
  42.5 7.2 %all-to-all-done.1 = f32[64,1,8]{2,1,0:T(1,128)S(1)} async-done(((f32[64,1,8]{2,1,0:T(1,128)}), f32[64,1,8]{2,1,0:T(1,128)S(1)}, u32[]{:S(2)}, u32[]{:S(2)}) %all-to-all-start.1) | async-done | bytes 2080 | tf_op jit(solution)/shard_map/all_to_all | solution.py:96
  49.7 4.7 all-to-all-start.2
  55.3 3.5 collective-permute-start
  60.7 3.2 collective-permute-done.2
  73.1 3.3 collective-permute-start.1
  100.7 4.8 collective-permute-done.9
  110.3 3.8 collective-permute-done.11
  118.7 3.8 collective-permute-done.13
  135.8 3.5 collective-permute-done.17
  142.7 41.9 %all-gather.3.cloned.1.call-done = f32[4,4,256,128]{3,2,1,0:T(8,128)} async-done(((f32[1,4,256,128]{3,2,1,0:T(8,128)}), f32[4,4,256,128]{3,2,1,0:T(8,128)}) %all-gather.3.cloned.1.call-update) | async-done | bytes 2097168 | tf_op jit(solution)/shard_map/all_gather | solution.py:141
  195.3 4.8 collective-permute-start.18
  202.1 3.0 collective-permute-done.19
  225.1 3.9 collective-permute-done.25
  232.3 80.5 %all-reduce.21 = (f32[]{:T(128)}, f32[]{:T(128)}) all-reduce(f32[]{:T(128)S(6)} %add.397, f32[]{:T(128)S(6)} %add.433), channel_id=1, replica_groups=mesh['mem'=4,'col'=64] {'mem','col'}, use_global_device_ids=true, to_apply=%region_9.10 | all-reduce | flops 2 | bytes 16 | tf_op jit(solution)/shard_map/psum | solution.py:128
  316.8 72.7 %psum.30 = f32[]{:T(128)} all-reduce(f32[]{:T(128)S(6)} %add.434), channel_id=1, replica_groups=mesh['mem'=4,'col'=64] {'mem','col'}, use_global_device_ids=true, to_apply=%region_17.18 | all-reduce | flops 1 | bytes 8 | tf_op jit(solution)/shard_map/psum | solution.py:150
  390.9 4.2 collective-permute-start.26
  397.3 3.0 collective-permute-done.27
  426.9 35.5 %all-gather.5.cloned.1.call-done = f32[4,4,256,128]{3,2,1,0:T(8,128)} async-done(((f32[1,4,256,128]{3,2,1,0:T(8,128)}), f32[4,4,256,128]{3,2,1,0:T(8,128)}) %all-gather.5.cloned.1.call-update) | async-done | bytes 2097168 | tf_op jit(solution)/shard_map/all_gather | solution.py:141
  469.2 3.5 scatter_custom_fusion.5
  478.8 4.8 collective-permute-start.34
  516.2 80.4 %psum.31 = f32[]{:T(128)} all-reduce(f32[]{:T(128)S(6)} %add.472), channel_id=1, replica_groups=mesh['mem'=4,'col'=64] {'mem','col'}, use_global_device_ids=true, to_apply=%region_22.23 | all-reduce | flops 1 | bytes 8 | tf_op jit(solution)/shard_map/psum | solution.py:148
  (220 shorter events, 179.8 us)
Async XLA Ops:
  13.3 22.4 %all-to-all-start = ((s32[64,1,8]{2,1,0:T(1,128)}), s32[64,1,8]{2,1,0:T(1,128)S(1)}, u32[]{:S(2)}, u32[]{:S(2)}) async-start(s32[64,1,8]{2,1,0:T(1,128)} %bitcast.6), calls=%async_computation | async-start | bytes 65536 | tf_op jit(solution)/shard_map/all_to_all | solution.py:93
  35.7 14.1 %all-to-all-start.1 = ((f32[64,1,8]{2,1,0:T(1,128)}), f32[64,1,8]{2,1,0:T(1,128)S(1)}, u32[]{:S(2)}, u32[]{:S(2)}) async-start(f32[64,1,8]{2,1,0:T(1,128)} %bitcast.8), calls=%async_computation.1 | async-start | bytes 65536 | tf_op jit(solution)/shard_map/all_to_all | solution.py:96
  49.7 17.7 %all-to-all-start.2 = ((f32[64,8,128]{2,1,0:T(8,128)}), f32[64,8,128]{2,1,0:T(8,128)S(1)}, u32[]{:S(2)}, u32[]{:S(2)}) async-start(f32[64,8,128]{2,1,0:T(8,128)} %bitcast.9), calls=%async_computation.2 | async-start | bytes 524288 | tf_op jit(solution)/shard_map/all_to_all | solution.py:86
  54.4 130.2 %all-gather.3.cloned.1.call-start = ((), (), s32[]{:S(2)}) async-start(), calls=%async_computation.3 | async-start | bytes 2621440 | tf_op jit(solution)/shard_map/all_gather | solution.py:141
  55.3 5.5 collective-permute-start
  58.8 5.2 collective-permute-start.2
  73.1 5.3 collective-permute-start.1
  76.4 5.0 collective-permute-start.3
  90.8 5.3 collective-permute-start.7
  98.3 7.2 %collective-permute-start.9 = (f32[8,1,256]{2,1,0:T(1,128)S(1)}, f32[8,1,256]{2,1,0:T(1,128)S(1)}, u32[]{:S(2)}, u32[]{:S(2)}) collective-permute-start(f32[8,1,256]{2,1,0:T(1,128)S(1)} %get-tuple-element.41), channel_id=1, source_target_pairs={{1,0},{2,1},{3,2},{4,3},{5,4},{6,5},{7,6},{8,7},{9,8},{10,9},{11,1... | collective-permute-start | bytes 24584 | tf_op jit(solution)/shard_map/ppermute | solution.py:18
  107.9 6.2 %collective-permute-start.11 = (f32[8,1,256]{2,1,0:T(1,128)S(1)}, f32[8,1,256]{2,1,0:T(1,128)S(1)}, u32[]{:S(2)}, u32[]{:S(2)}) collective-permute-start(f32[8,1,256]{2,1,0:T(1,128)S(1)} %get-tuple-element.39), channel_id=1, source_target_pairs={{1,0},{2,1},{3,2},{4,3},{5,4},{6,5},{7,6},{8,7},{9,8},{10,9},{11,1... | collective-permute-start | bytes 24584 | tf_op jit(solution)/shard_map/ppermute | solution.py:18
  116.3 6.2 %collective-permute-start.13 = (f32[8,1,256]{2,1,0:T(1,128)S(1)}, f32[8,1,256]{2,1,0:T(1,128)S(1)}, u32[]{:S(2)}, u32[]{:S(2)}) collective-permute-start(f32[8,1,256]{2,1,0:T(1,128)S(1)} %get-tuple-element.37), channel_id=1, source_target_pairs={{1,0},{2,1},{3,2},{4,3},{5,4},{6,5},{7,6},{8,7},{9,8},{10,9},{11,1... | collective-permute-start | bytes 24584 | tf_op jit(solution)/shard_map/ppermute | solution.py:18
  122.7 5.2 collective-permute-start.14
  124.7 6.2 %collective-permute-start.15 = (f32[8,1,256]{2,1,0:T(1,128)S(1)}, f32[8,1,256]{2,1,0:T(1,128)S(1)}, u32[]{:S(2)}, u32[]{:S(2)}) collective-permute-start(f32[8,1,256]{2,1,0:T(1,128)S(1)} %get-tuple-element.35), channel_id=1, source_target_pairs={{1,0},{2,1},{3,2},{4,3},{5,4},{6,5},{7,6},{8,7},{9,8},{10,9},{11,1... | collective-permute-start | bytes 24584 | tf_op jit(solution)/shard_map/ppermute | solution.py:18
  133.1 6.2 %collective-permute-start.17 = (f32[8,1,256]{2,1,0:T(1,128)S(1)}, f32[8,1,256]{2,1,0:T(1,128)S(1)}, u32[]{:S(2)}, u32[]{:S(2)}) collective-permute-start(f32[8,1,256]{2,1,0:T(1,128)S(1)} %get-tuple-element.33), channel_id=1, source_target_pairs={{1,0},{2,1},{3,2},{4,3},{5,4},{6,5},{7,6},{8,7},{9,8},{10,9},{11,1... | collective-permute-start | bytes 24584 | tf_op jit(solution)/shard_map/ppermute | solution.py:18
  142.6 319.8 %all-gather.5.cloned.1.call-start = ((), (), s32[]{:S(2)}) async-start(), calls=%async_computation.4 | async-start | bytes 2621440 | tf_op jit(solution)/shard_map/all_gather | solution.py:141
  195.3 6.8 %collective-permute-start.18 = (f32[8,1,256]{2,1,0:T(1,128)S(1)}, f32[8,1,256]{2,1,0:T(1,128)S(1)}, u32[]{:S(2)}, u32[]{:S(2)}) collective-permute-start(f32[8,1,256]{2,1,0:T(1,128)S(1)} %get-tuple-element.30), channel_id=1, source_target_pairs={{0,1},{1,2},{2,3},{3,4},{4,5},{5,6},{6,7},{7,8},{8,9},{9,10},{10,1... | collective-permute-start | bytes 24584 | tf_op jit(solution)/shard_map/ppermute | solution.py:15
  219.8 5.3 collective-permute-start.24
  221.7 7.2 %collective-permute-start.25 = (f32[8,1,256]{2,1,0:T(1,128)S(1)}, f32[8,1,256]{2,1,0:T(1,128)S(1)}, u32[]{:S(2)}, u32[]{:S(2)}) collective-permute-start(f32[8,1,256]{2,1,0:T(1,128)S(1)} %get-tuple-element.25), channel_id=1, source_target_pairs={{1,0},{2,1},{3,2},{4,3},{5,4},{6,5},{7,6},{8,7},{9,8},{10,9},{11,1... | collective-permute-start | bytes 24584 | tf_op jit(solution)/shard_map/ppermute | solution.py:18
  390.9 6.4 %collective-permute-start.26 = (f32[8,1,256]{2,1,0:T(1,128)S(1)}, f32[8,1,256]{2,1,0:T(1,128)S(1)}, u32[]{:S(2)}, u32[]{:S(2)}) collective-permute-start(f32[8,1,256]{2,1,0:T(1,128)S(1)} %get-tuple-element.22), channel_id=1, source_target_pairs={{0,1},{1,2},{2,3},{3,4},{4,5},{5,6},{6,7},{7,8},{8,9},{9,10},{10,1... | collective-permute-start | bytes 24584 | tf_op jit(solution)/shard_map/ppermute | solution.py:15
  395.1 5.2 collective-permute-start.27
  478.8 6.8 %collective-permute-start.34 = (f32[8,1,256]{2,1,0:T(1,128)S(1)}, f32[8,1,256]{2,1,0:T(1,128)S(1)}, u32[]{:S(2)}, u32[]{:S(2)}) collective-permute-start(f32[8,1,256]{2,1,0:T(1,128)S(1)} %get-tuple-element.14), channel_id=1, source_target_pairs={{0,1},{1,2},{2,3},{3,4},{4,5},{5,6},{6,7},{7,8},{8,9},{9,10},{10,1... | collective-permute-start | bytes 24584 | tf_op jit(solution)/shard_map/ppermute | solution.py:15
  504.9 6.1 %collective-permute-start.40 = (f32[8,1,256]{2,1,0:T(1,128)S(1)}, f32[8,1,256]{2,1,0:T(1,128)S(1)}, u32[]{:S(2)}, u32[]{:S(2)}) collective-permute-start(f32[8,1,256]{2,1,0:T(1,128)S(1)} %get-tuple-element.8), channel_id=1, source_target_pairs={{0,1},{1,2},{2,3},{3,4},{4,5},{5,6},{6,7},{7,8},{8,9},{9,10},{10,1... | collective-permute-start | bytes 24584 | tf_op jit(solution)/shard_map/ppermute | solution.py:15
  506.8 7.2 %collective-permute-start.41 = (f32[8,1,256]{2,1,0:T(1,128)S(1)}, f32[8,1,256]{2,1,0:T(1,128)S(1)}, u32[]{:S(2)}, u32[]{:S(2)}) collective-permute-start(f32[8,1,256]{2,1,0:T(1,128)S(1)} %get-tuple-element.9), channel_id=1, source_target_pairs={{1,0},{2,1},{3,2},{4,3},{5,4},{6,5},{7,6},{8,7},{9,8},{10,9},{11,1... | collective-permute-start | bytes 24584 | tf_op jit(solution)/shard_map/ppermute | solution.py:18
  (33 other events, 609.4 us)
Sparse Core Ops, SparseCore 0:
  142.7 41.8 all-gather.2
  427.0 35.3 all-gather.4
